TPU v7x, 32 devices: a whole 2x2x4 slice. The times are simulated.
32 devices in a mesh: row: 8 (over z, y), col: 4 (over x, core).
Axes of the slice: x: 2, y: 2, z: 4, core: 2. Of those that a mesh axis runs over, the one named last changes fastest.
Arguments:
- tokens: bfloat16 [2048, 4096], P('row', 'col'), may hold values from -6 to 6
- cotangent: bfloat16 [2048, 4096], P('row', 'col'), may hold values from -1.25 to 1.25
- w_up: float32 [4096, 12288], P('row', 'col'), may hold values from -0.1875 to 0.1875
- w_down: float32 [4096, 12288], P('row', 'col'), may hold values from -0.109375 to 0.109375
- mask_up: int32 [32, 96], P('row', 'col'), may hold values from 0 to 1, as said below
- mask_down: int32 [32, 96], P('row', 'col'), may hold values from 0 to 1, as said below
- moment_up: float32 [4096, 12288], P('row', 'col'), may hold values from -1.5 to 1.5
- second_up: float32 [4096, 12288], P('row', 'col'), may hold values from 0.01 to 0.2
- moment_down: float32 [4096, 12288], P('row', 'col'), may hold values from -1.5 to 1.5
- second_down: float32 [4096, 12288], P('row', 'col'), may hold values from 0.01 to 0.2
Outputs:
- token_grad: bfloat16 [2048, 4096], P('row', 'col')
- new_up: float32 [4096, 12288], P('row', 'col')
- new_moment_up: float32 [4096, 12288], P('row', 'col')
- new_second_up: float32 [4096, 12288], P('row', 'col')
- new_down: float32 [4096, 12288], P('row', 'col')
- new_moment_down: float32 [4096, 12288], P('row', 'col')
- new_second_down: float32 [4096, 12288], P('row', 'col')
Inputs may be any that keep to these rules, and one draw needn't show every extreme that they name: `mask_up`: 1 where the 128 x 128 block of the up projection is kept, else 0. Each tile of 4 x 24 blocks (the blocks of one device) holds at least 1 and at most 48 kept blocks, and some tile holds exactly 48. `mask_down`: 1 where the 128 x 128 block of the down projection is kept, else 0. Each tile of 4 x 24 blocks (the blocks of one device) holds at least 1 and at most 48 kept blocks, and some tile holds exactly 48.
All inputs are finite; a program needn't handle non-finite values.
Results may differ from a plain program's by a relative error of at most 0.018.
Values may be sent and summed in bfloat16 or wider, within the bound.
No kernel may reach another device: no remote copies, remote signals or barrier semaphores. Data moves between devices by JAX's collectives and lax.ppermute only.
A program may use at most 320 MiB of HBM per device.

v0:
```python
import jax
import jax.numpy as jnp
from jax import lax
from jax.sharding import PartitionSpec as P

inv_root_two = 0.7071067811865476
inv_root_two_pi = 0.3989422804014327
learn_rate = 0.001
bias_first = 1.0 - 0.9**10
bias_second = 1.0 - 0.95**10


def expand_mask(mask, block):
    blocks_r, blocks_c = mask.shape
    values = mask.astype(jnp.float32)[:, None, :, None]
    values = jnp.broadcast_to(values, (blocks_r, block, blocks_c, block))
    return values.reshape(blocks_r * block, blocks_c * block)


def gelu_parts(preact):
    normal_cdf = 0.5 * (1.0 + lax.erf(preact * inv_root_two))
    density = jnp.exp(-0.5 * preact * preact) * inv_root_two_pi
    return (preact * normal_cdf, normal_cdf + preact * density)


def adam_update(weight, moment, second, grad):
    moment_new = 0.9 * moment + 0.1 * grad
    second_new = 0.95 * second + 0.05 * grad * grad
    step_size = moment_new / bias_first / (jnp.sqrt(second_new / bias_second) + 1e-08)
    return (weight - learn_rate * step_size, moment_new, second_new)


def token_product(rows_full, other):
    return lax.dot_general(
        rows_full, other, (((0,), (0,)), ((), ())), preferred_element_type=jnp.float32
    )


def shards(
    tokens,
    cotangent,
    w_up,
    w_down,
    mask_up,
    mask_down,
    moment_up,
    second_up,
    moment_down,
    second_down,
):
    block = w_up.shape[0] // mask_up.shape[0]
    keep_up = expand_mask(mask_up, block)
    keep_down = expand_mask(mask_down, block)
    up_used = (w_up * keep_up).astype(jnp.bfloat16)
    down_used = (w_down * keep_down).astype(jnp.bfloat16)
    features, cot_rows = (
        lax.all_gather(tokens, "col", axis=1, tiled=True),
        lax.all_gather(cotangent, "col", axis=1, tiled=True),
    )
    up_whole = lax.all_gather(up_used, "row", axis=0, tiled=True)
    preact = jnp.dot(features, up_whole, preferred_element_type=jnp.float32)
    act_grad = jnp.dot(
        cot_rows,
        lax.all_gather(down_used, "row", axis=0, tiled=True),
        preferred_element_type=jnp.float32,
    )
    gelu_value, gelu_slope = gelu_parts(preact)
    activation = gelu_value.astype(jnp.bfloat16)
    pre_grad = (act_grad * gelu_slope).astype(jnp.bfloat16)
    partial_tokens = lax.dot_general(
        pre_grad, up_whole, (((1,), (1,)), ((), ())), preferred_element_type=jnp.float32
    )
    summed_down = lax.psum_scatter(
        token_product(cot_rows, activation).astype(jnp.bfloat16),
        "row",
        scatter_dimension=0,
        tiled=True,
    ).astype(jnp.float32)
    summed_up = lax.psum_scatter(
        token_product(features, pre_grad).astype(jnp.bfloat16),
        "row",
        scatter_dimension=0,
        tiled=True,
    ).astype(jnp.float32)
    token_grad = lax.psum_scatter(
        partial_tokens.astype(jnp.bfloat16), "col", scatter_dimension=1, tiled=True
    )
    grad_up = keep_up * summed_up
    grad_down = keep_down * summed_down
    new_up, new_moment_up, new_second_up = adam_update(w_up, moment_up, second_up, grad_up)
    new_down, new_moment_down, new_second_down = adam_update(
        w_down, moment_down, second_down, grad_down
    )
    return (
        token_grad,
        new_up,
        new_moment_up,
        new_second_up,
        new_down,
        new_moment_down,
        new_second_down,
    )


def solution(mesh):
    return jax.shard_map(
        shards,
        mesh=mesh,
        in_specs=(
            P("row", "col"),
            P("row", "col"),
            P("row", "col"),
            P("row", "col"),
            P("row", "col"),
            P("row", "col"),
            P("row", "col"),
            P("row", "col"),
            P("row", "col"),
            P("row", "col"),
        ),
        out_specs=(
            P("row", "col"),
            P("row", "col"),
            P("row", "col"),
            P("row", "col"),
            P("row", "col"),
            P("row", "col"),
            P("row", "col"),
        ),
        check_vma=False,
    )
```

profile of v0, /device:TPU:0, one launch (start us, length us, event | category | flops | bytes accessed | tf_op | source)
XLA Modules:
  0.0 1936.0 jit_solution(5846292603456907985)
XLA Ops:
  8.7 6.6 copy.20
  24.0 10.8 all-gather.11.cloned.1.call-done
  34.9 482.6 %all-gather.9.cloned.1.call-done = bf16[4096,3072]{0,1:T(8,128)(2,1)} async-done(((bf16[512,3072]{0,1:T(8,128)(2,1)}), bf16[4096,3072]{0,1:T(8,128)(2,1)}) %all-gather.9.cloned.1.call-update) | async-done | bytes 25165840 | tf_op jit(solution)/shard_map/all_gather | solution.py:60
  517.5 12.5 convolution_bitcast_fusion
  530.0 11.6 all-gather.7.cloned.1.call-done
  541.6 13.3 convert_bitcast_fusion
  562.2 7.0 copy.24
  569.3 6.6 copy.25
  575.8 383.7 %reduce-scatter.8.cloned.1.call-done = bf16[512,3072]{0,1:T(8,128)(2,1)} async-done(((bf16[4096,3072]{0,1:T(8,128)(2,1)}), bf16[512,3072]{0,1:T(8,128)(2,1)}) %reduce-scatter.8.cloned.1.call-update) | async-done | bytes 3145744 | tf_op jit(solution)/shard_map/reduce_scatter | solution.py:73
  964.6 15.1 multiply_subtract_fusion
  980.0 479.4 %all-gather.5.cloned.1.call-done = bf16[4096,3072]{0,1:T(8,128)(2,1)} async-done(((bf16[512,3072]{0,1:T(8,128)(2,1)}), bf16[4096,3072]{0,1:T(8,128)(2,1)}) %all-gather.5.cloned.1.call-update) | async-done | bytes 25165840 | tf_op jit(solution)/shard_map/all_gather | solution.py:64
  1459.4 13.6 fusion.5
  1473.1 13.3 convert_bitcast_fusion.1
  1486.7 14.3 convolution_convert_fusion
  1501.1 6.6 copy.21
  1507.7 6.6 copy.22
  1514.3 6.6 copy.30
  1520.8 6.6 copy.31
  1527.4 6.6 copy.32
  1534.0 356.8 %reduce-scatter.6.cloned.1.call-done = bf16[512,3072]{0,1:T(8,128)(2,1)} async-done(((bf16[4096,3072]{0,1:T(8,128)(2,1)}), bf16[512,3072]{0,1:T(8,128)(2,1)}) %reduce-scatter.6.cloned.1.call-update) | async-done | bytes 3145744 | tf_op jit(solution)/shard_map/reduce_scatter | solution.py:79
  1890.8 18.3 multiply_subtract_fusion.1
  1909.1 6.9 copy.27
  1916.0 6.6 copy.28
  1922.6 6.6 copy.29
  (33 shorter events, 23.2 us)
Async XLA Ops:
  7.2 27.7 %all-gather.11.cloned.1.call-start = ((), (), s32[]{:S(2)}) async-start(), calls=%async_computation.6 | async-start | bytes 2621440 | tf_op jit(solution)/shard_map/all_gather | solution.py:57
  7.9 509.6 %all-gather.9.cloned.1.call-start = ((), (), s32[]{:S(2)}) async-start(), calls=%async_computation.5 | async-start | bytes 28311552 | tf_op jit(solution)/shard_map/all_gather | solution.py:60
  15.3 5.1 copy-start
  16.2 3.2 copy-start.1
  23.2 518.4 %all-gather.7.cloned.1.call-start = ((), (), s32[]{:S(2)}) async-start(), calls=%async_computation.4 | async-start | bytes 2621440 | tf_op jit(solution)/shard_map/all_gather | solution.py:58
  24.0 935.5 %reduce-scatter.8.cloned.1.call-start = ((), (), s32[]{:S(2)}) async-start(), calls=%async_computation.9 | async-start | bytes 28311552 | tf_op jit(solution)/shard_map/reduce_scatter | solution.py:73
  530.0 24.9 %copy-start.3 = (f32[256,3072]{0,1:T(8,128)}, f32[256,3072]{0,1:T(8,128)S(1)}, u32[]{:S(2)}) copy-start(f32[256,3072]{0,1:T(8,128)S(1)} %convolution_bitcast_fusion) | copy-start | bytes 9437188
  554.9 0.7 copy-start.4
  554.9 904.5 %all-gather.5.cloned.1.call-start = ((), (), s32[]{:S(2)}) async-start(), calls=%async_computation.3 | async-start | bytes 28311552 | tf_op jit(solution)/shard_map/all_gather | solution.py:64
  959.5 5.1 copy-start.2
  979.8 911.0 %reduce-scatter.6.cloned.1.call-start = ((), (), s32[]{:S(2)}) async-start(), calls=%async_computation.8 | async-start | bytes 28311552 | tf_op jit(solution)/shard_map/reduce_scatter | solution.py:79
  1486.4 442.7 %reduce-scatter.4.cloned.1.call-start = ((), (), s32[]{:S(2)}) async-start(), calls=%async_computation.7 | async-start | bytes 2621440 | tf_op jit(solution)/shard_map/reduce_scatter | solution.py:85
Sparse Core Ops, SparseCore 0:
  9.6 25.2 all-gather.10
  37.0 480.4 all-gather.8
  519.0 22.5 all-gather.6
  555.1 404.4 reduce-scatter.7
  979.9 479.5 all-gather.4
  1486.5 404.2 reduce-scatter.5
  1893.9 30.5 reduce-scatter.3
where the time goes:
time: 1940 us
  waiting for transfers between devices  1730 us (89%)
  local copies, waits for them, and re-layouts  90.5 us (5%)
  matrix products  67.1 us (3%)
  other arithmetic  37 us (2%)
    all_gather x1, waiting for transfers between devices, shards(): up_whole = lax.all_gather(up_used, 'row', axis=0, tiled=True)  483 us
    all_gather x1, waiting for transfers between devices, shards(): lax.all_gather(down_used, 'row', axis=0, tiled=True)  479 us
    reduce_scatter x1, waiting for transfers between devices, shards(): lax.psum_scatter(token_product(cot_rows, activation).astype(jnp.bfloat16)...  384 us
    reduce_scatter x1, waiting for transfers between devices, shards(): lax.psum_scatter(token_product(features, pre_grad).astype(jnp.bfloat16),...  357 us
    unnamed x22, local copies, waits for them, and re-layouts  85.3 us
  transfers between devices with their start and end apart: 7, of which 6 were waited for; matrix products, arithmetic and copies ran while one was open for 7% of the time, Pallas kernels for 0%

commit v1 on v0

--- a/solution.py
+++ b/solution.py
@@ -57,7 +57,15 @@
         lax.all_gather(tokens, "col", axis=1, tiled=True),
         lax.all_gather(cotangent, "col", axis=1, tiled=True),
     )
-    up_whole = lax.all_gather(up_used, "row", axis=0, tiled=True)
+    ways, here = (lax.axis_size("row"), lax.axis_index("row"))
+    grown, reach = (up_used, 1)
+    while reach < ways:
+        theirs = lax.ppermute(grown, "row", [(d, d ^ reach) for d in range(ways)])
+        mine_first = jnp.concatenate([grown, theirs], axis=0)
+        theirs_first = jnp.concatenate([theirs, grown], axis=0)
+        grown = jnp.where(here & reach == 0, mine_first, theirs_first)
+        reach = 2 * reach
+    up_whole = grown
     preact = jnp.dot(features, up_whole, preferred_element_type=jnp.float32)
     act_grad = jnp.dot(
         cot_rows,

time: 1940 us -> 2210 us (1.14)
  waiting for transfers between devices: 1730 us -> 1950 us
  other arithmetic: 37 us -> 60.2 us
    ppermute x0 -> x3, waiting for transfers between devices: none -> 720 us  [shards(): theirs = lax.ppermute(grown, 'row', [(d, d ^ reach) for d in range(ways)])]
    all_gather x1 -> x0, waiting for transfers between devices: 483 us -> none  [shards(): up_whole = lax.all_gather(up_used, 'row', axis=0, tiled=True)]
    select_n x0 -> x2, other arithmetic: none -> 24.3 us  [shards(): grown = jnp.where(here & reach == 0, mine_first, theirs_first)]
    unnamed x22 -> x24, local copies, waits for them, and re-layouts: 85.3 us -> 85.3 us
  transfers between devices with their start and end apart: 7 -> 9, of which waited for: 6 -> 7; matrix products, arithmetic and copies ran while one was open for 7% -> 6% of each run, Pallas kernels for 0% -> 0%
where the time goes in v1:
time: 2210 us
  waiting for transfers between devices  1950 us (88%)
  local copies, waits for them, and re-layouts  90.4 us (4%)
  matrix products  89.1 us (4%)
  other arithmetic  60.2 us (3%)
    ppermute x3, waiting for transfers between devices, shards(): theirs = lax.ppermute(grown, 'row', [(d, d ^ reach) for d in range(ways)])  720 us
    all_gather x1, waiting for transfers between devices, shards(): lax.all_gather(down_used, 'row', axis=0, tiled=True)  479 us
    reduce_scatter x1, waiting for transfers between devices, shards(): lax.psum_scatter(token_product(cot_rows, activation).astype(jnp.bfloat16)...  384 us
    reduce_scatter x1, waiting for transfers between devices, shards(): lax.psum_scatter(token_product(features, pre_grad).astype(jnp.bfloat16),...  346 us
    unnamed x24, local copies, waits for them, and re-layouts  85.3 us
  transfers between devices with their start and end apart: 9, of which 7 were waited for; matrix products, arithmetic and copies ran while one was open for 6% of the time, Pallas kernels for 0%

profile of v1, /device:TPU:0, one launch (start us, length us, event | category | flops | bytes accessed | tf_op | source)
XLA Modules:
  0.0 2213.8 jit_solution(8141045959085610564)
XLA Ops:
  24.4 68.2 %collective-permute-done = bf16[512,3072]{0,1:T(8,128)(2,1)} collective-permute-done((bf16[512,3072]{0,1:T(8,128)(2,1)S(1)}, bf16[512,3072]{0,1:T(8,128)(2,1)}, u32[]{:S(2)}, u32[]{:S(2)}) %collective-permute-start) | collective-permute-done | bytes 3145760 | tf_op jit(solution)/shard_map/ppermute | solution.py:63
  92.6 8.1 maximum_select_fusion.2
  102.5 135.2 %collective-permute-done.1 = bf16[1024,3072]{0,1:T(8,128)(2,1)} collective-permute-done((bf16[1024,3072]{0,1:T(8,128)(2,1)}, bf16[1024,3072]{0,1:T(8,128)(2,1)}, u32[]{:S(2)}, u32[]{:S(2)}) %collective-permute-start.1) | collective-permute-done | bytes 6291488 | tf_op jit(solution)/shard_map/ppermute | solution.py:63
  237.7 16.2 maximum_select_fusion.1
  257.3 21.2 all-gather.8.cloned.1.call-done
  278.4 517.0 %collective-permute-done.2 = bf16[2048,3072]{0,1:T(8,128)(2,1)} collective-permute-done((bf16[2048,3072]{0,1:T(8,128)(2,1)}, bf16[2048,3072]{0,1:T(8,128)(2,1)}, u32[]{:S(2)}, u32[]{:S(2)}) %collective-permute-start.2) | collective-permute-done | bytes 12582944 | tf_op jit(solution)/shard_map/ppermute | solution.py:63
  795.4 21.8 fusion.5
  817.3 14.4 convert_bitcast_fusion
  839.0 7.0 copy.24
  846.1 6.6 copy.25
  852.6 384.2 %reduce-scatter.8.cloned.1.call-done = bf16[512,3072]{0,1:T(8,128)(2,1)} async-done(((bf16[4096,3072]{0,1:T(8,128)(2,1)}), bf16[512,3072]{0,1:T(8,128)(2,1)}) %reduce-scatter.8.cloned.1.call-update) | async-done | bytes 3145744 | tf_op jit(solution)/shard_map/reduce_scatter | solution.py:81
  1241.8 15.1 multiply_subtract_fusion
  1257.3 479.4 %all-gather.4.cloned.1.call-done = bf16[4096,3072]{0,1:T(8,128)(2,1)} async-done(((bf16[512,3072]{0,1:T(8,128)(2,1)}), bf16[4096,3072]{0,1:T(8,128)(2,1)}) %all-gather.4.cloned.1.call-update) | async-done | bytes 25165840 | tf_op jit(solution)/shard_map/all_gather | solution.py:72
  1736.7 13.4 convolution_bitcast_fusion
  1750.1 14.1 convert_bitcast_fusion.1
  1764.5 25.4 %convolution_convert_fusion = bf16[256,4096]{1,0:T(8,128)(2,1)} fusion(bf16[2048,3072]{0,1:T(8,128)(2,1)} %collective-permute-done.2, bf16[2048,3072]{0,1:T(8,128)(2,1)} %maximum_select_fusion.1, pred[]{:T(512)S(6)} %eq.9, f32[256,3072]{0,1:T(8,128)} %convolution_bitcast_fusion, f32[256,3072]{0,1:T(8,128)S(1)} %copy-done.4), kind=kOutput, calls=%fused_computation.19 | convolution fusion | flops 6564610048 | bytes 33554432 | tf_op jit(solution)/shard_map/dot_general | solution.py:78
  1790.0 6.6 copy.21
  1796.5 6.6 copy.22
  1803.2 6.6 copy.30
  1809.8 6.6 copy.31
  1816.3 6.6 copy.32
  1823.0 345.7 %reduce-scatter.6.cloned.1.call-done = bf16[512,3072]{0,1:T(8,128)(2,1)} async-done(((bf16[4096,3072]{0,1:T(8,128)(2,1)}), bf16[512,3072]{0,1:T(8,128)(2,1)}) %reduce-scatter.6.cloned.1.call-update) | async-done | bytes 3145744 | tf_op jit(solution)/shard_map/reduce_scatter | solution.py:87
  2168.7 18.3 multiply_subtract_fusion.1
  2187.0 6.9 copy.27
  (40 shorter events, 48.4 us)
Async XLA Ops:
  7.2 271.3 %all-gather.8.cloned.1.call-start = ((), (), s32[]{:S(2)}) async-start(), calls=%async_computation.5 | async-start | bytes 2621440 | tf_op jit(solution)/shard_map/all_gather | solution.py:57
  14.5 5.1 copy-start
  15.4 6.0 copy-start.1
  21.4 71.2 %collective-permute-start = (bf16[512,3072]{0,1:T(8,128)(2,1)S(1)}, bf16[512,3072]{0,1:T(8,128)(2,1)}, u32[]{:S(2)}, u32[]{:S(2)}) collective-permute-start(bf16[512,3072]{0,1:T(8,128)(2,1)S(1)} %fusion.2), channel_id=1, source_target_pairs={{0,4},{4,0},{8,12},{12,8},{16,20},{20,16},{24,28},{28,24},{1,5},{5... | collective-permute-start | bytes 9437192 | tf_op jit(solution)/shard_map/ppermute | solution.py:63
  100.7 137.0 %collective-permute-start.1 = (bf16[1024,3072]{0,1:T(8,128)(2,1)}, bf16[1024,3072]{0,1:T(8,128)(2,1)}, u32[]{:S(2)}, u32[]{:S(2)}) collective-permute-start(bf16[1024,3072]{0,1:T(8,128)(2,1)} %maximum_select_fusion.2), channel_id=1, source_target_pairs={{0,8},{4,12},{8,0},{12,4},{16,24},{20,28},{24,16},{28,20},{1,9},{5... | collective-permute-start | bytes 18874376 | tf_op jit(solution)/shard_map/ppermute | solution.py:63
  253.9 541.5 %collective-permute-start.2 = (bf16[2048,3072]{0,1:T(8,128)(2,1)}, bf16[2048,3072]{0,1:T(8,128)(2,1)}, u32[]{:S(2)}, u32[]{:S(2)}) collective-permute-start(bf16[2048,3072]{0,1:T(8,128)(2,1)} %maximum_select_fusion.1), channel_id=1, source_target_pairs={{0,16},{4,20},{8,24},{12,28},{16,0},{20,4},{24,8},{28,12},{1,17},{... | collective-permute-start | bytes 37748744 | tf_op jit(solution)/shard_map/ppermute | solution.py:63
  256.5 560.8 %all-gather.6.cloned.1.call-start = ((), (), s32[]{:S(2)}) async-start(), calls=%async_computation.4 | async-start | bytes 2621440 | tf_op jit(solution)/shard_map/all_gather | solution.py:58
  257.2 979.6 %reduce-scatter.8.cloned.1.call-start = ((), (), s32[]{:S(2)}) async-start(), calls=%async_computation.8 | async-start | bytes 28311552 | tf_op jit(solution)/shard_map/reduce_scatter | solution.py:81
  817.2 14.4 copy-start.3
  831.7 0.7 copy-start.5
  831.7 905.0 %all-gather.4.cloned.1.call-start = ((), (), s32[]{:S(2)}) async-start(), calls=%async_computation.3 | async-start | bytes 28311552 | tf_op jit(solution)/shard_map/all_gather | solution.py:72
  1236.8 5.1 copy-start.2
  1257.0 493.1 %copy-start.4 = (f32[256,3072]{0,1:T(8,128)S(1)}, f32[256,3072]{0,1:T(8,128)}, u32[]{:S(2)}) copy-start(f32[256,3072]{0,1:T(8,128)} %copy-done.3) | copy-start | bytes 9437188
  1257.0 911.7 %reduce-scatter.6.cloned.1.call-start = ((), (), s32[]{:S(2)}) async-start(), calls=%async_computation.7 | async-start | bytes 28311552 | tf_op jit(solution)/shard_map/reduce_scatter | solution.py:87
  1764.2 442.8 %reduce-scatter.4.cloned.1.call-start = ((), (), s32[]{:S(2)}) async-start(), calls=%async_computation.6 | async-start | bytes 2621440 | tf_op jit(solution)/shard_map/reduce_scatter | solution.py:93
Sparse Core Ops, SparseCore 0:
  256.6 21.7 all-gather.7
  280.0 22.5 all-gather.5
  831.8 404.9 reduce-scatter.7
  1257.1 479.5 all-gather.3
  1764.4 404.2 reduce-scatter.5
  2171.7 30.5 reduce-scatter.3
